TPU v7x, 32 devices: a whole 2x2x4 slice. The times are simulated.
32 devices in a mesh: sec: 4 (over y, x), tile: 8 (over z, core).
Axes of the slice: x: 2, y: 2, z: 4, core: 2. Of those that a mesh axis runs over, the one named last changes fastest.
Arguments:
- tracers: bfloat16 [4, 72, 32, 1024], P(None, None, 'sec', 'tile'), may hold values from -6 to 6
- courant: bfloat16 [2, 72, 32, 1024], P(None, None, 'sec', 'tile'), may hold values from -0.44921875 to 0.44921875
- destination: int32 [32, 8], P(('sec', 'tile')), may hold values from 0 to 7, each once within a row
- diffusion: bfloat16 [32, 72, 72], P(('sec', 'tile')), may hold values from 0 to 1.25
- band: int32 [32], P(('sec', 'tile')), may hold values from 0 to 15
- band_table: bfloat16 [16, 72, 72], replicated, may hold values from -0.75 to 0.75
Outputs:
- column_state: bfloat16 [4, 72, 256, 128], P(None, None, ('sec', 'tile'))
Inputs may be any that keep to these rules, and one draw needn't show every extreme that they name: Each row of destination names every column block of its group once.
All inputs are finite; a program needn't handle non-finite values.
Results may differ from a plain program's by a relative error of at most 0.0066.
Values may be sent and summed in bfloat16 or wider, within the bound.
No kernel may reach another device: no remote copies, remote signals or barrier semaphores. Data moves between devices by JAX's collectives and lax.ppermute only.
A program may use at most 128 MiB of HBM per device.

v0:
```python
import jax
import jax.numpy as jnp
from jax import lax
from jax.sharding import PartitionSpec as P

STEPS = 3


def with_halo(cells, sides, width):
    for axis, dim in sides:
        count = lax.axis_size(axis)
        head = lax.slice_in_dim(cells, 0, width, axis=dim)
        tail = lax.slice_in_dim(cells, cells.shape[dim] - width, cells.shape[dim], axis=dim)
        cells = jnp.concatenate(
            [
                lax.ppermute(tail, axis, [(i, (i + 1) % count) for i in range(count)]),
                cells,
                lax.ppermute(head, axis, [((i + 1) % count, i) for i in range(count)]),
            ],
            axis=dim,
        )
    return cells


def advect_tile(padded, courant):
    centre = padded[:, :, 1:-1, 1:-1].astype(jnp.float32)
    north = padded[:, :, 2:, 1:-1].astype(jnp.float32)
    south = padded[:, :, :-2, 1:-1].astype(jnp.float32)
    east = padded[:, :, 1:-1, 2:].astype(jnp.float32)
    west = padded[:, :, 1:-1, :-2].astype(jnp.float32)
    cx = courant[0].astype(jnp.float32)
    cy = courant[1].astype(jnp.float32)
    out = centre - 0.5 * cx * (north - south) + 0.5 * cx * cx * (north - 2.0 * centre + south)
    out = out - 0.5 * cy * (east - west) + 0.5 * cy * cy * (east - 2.0 * centre + west)
    return out.astype(jnp.bfloat16)


def substep(field, courant):
    padded = with_halo(field, (("sec", 2), ("tile", 3)), 1)
    return advect_tile(padded, courant)


def per_device(tracers, courant, destination, diffusion, band, band_table):
    advected = tracers
    for step in range(STEPS):
        advected = substep(advected, courant)
    order = jnp.argsort(destination[0])
    band_count = band_table.shape[0]
    ordered = jnp.take(advected, order, axis=2)
    received = lax.all_to_all(ordered, "tile", split_axis=2, concat_axis=2, tiled=True)
    inverse = diffusion[0]
    diffused = jnp.einsum("kl,tlxy->tkxy", inverse, received, preferred_element_type=jnp.float32)
    diffused16 = diffused.astype(jnp.bfloat16)
    picked = (jnp.arange(band_count, dtype=jnp.int32) == band[0])[:, None, None]
    radiation = jnp.sum(jnp.where(picked, band_table, jnp.zeros_like(band_table)), axis=0)
    heating = jnp.einsum("kl,tlxy->tkxy", radiation, diffused16, preferred_element_type=jnp.float32)
    return (diffused + heating).astype(jnp.bfloat16)


def solution(mesh):
    placed = (
        P(None, None, "sec", "tile"),
        P(None, None, "sec", "tile"),
        P(("sec", "tile"), None),
        P(("sec", "tile"), None, None),
        P(("sec", "tile")),
        P(),
    )
    return jax.shard_map(
        per_device,
        mesh=mesh,
        in_specs=placed,
        out_specs=P(None, None, ("sec", "tile"), None),
        check_vma=False,
    )
```

profile of v0, /device:TPU:0, one launch (start us, length us, event | category | flops | bytes accessed | tf_op | source)
XLA Modules:
  0.0 81.5 jit_solution(5658749465886377989)
XLA Ops:
  0.0 1.2 %copy.20 = bf16[4,72,8,128]{3,1,2,0:T(8,128)(2,1)S(1)} copy(bf16[4,72,8,128]{3,2,1,0:T(8,128)(2,1)} %param.6) | data formatting | bytes 1179648 | tf_op args[0]
  1.2 3.0 %collective-permute-start.1 = (bf16[4,72,1,128]{3,1,2,0:T(8,128)(2,1)S(1)}, bf16[4,72,1,128]{3,1,2,0:T(8,128)(2,1)S(1)}, u32[]{:S(2)}, u32[]{:S(2)}) collective-permute-start(bf16[4,72,1,128]{3,1,2,0:T(8,128)(2,1)S(1)} %get-tuple-element.18), channel_id=1, source_target_pairs={{0,8},{8,16},{16,24},{24,0},{1,9},{9,17},{17,25},{25,1},{2,10},{10... | collective-permute-start | bytes 221192 | tf_op jit(solution)/shard_map/ppermute | solution.py:16
  4.2 1.0 %collective-permute-start = (bf16[4,72,1,128]{3,1,2,0:T(8,128)(2,1)S(1)}, bf16[4,72,1,128]{3,1,2,0:T(8,128)(2,1)S(1)}, u32[]{:S(2)}, u32[]{:S(2)}) collective-permute-start(bf16[4,72,1,128]{3,1,2,0:T(8,128)(2,1)S(1)} %get-tuple-element.17), channel_id=1, source_target_pairs={{8,0},{16,8},{24,16},{0,24},{9,1},{17,9},{25,17},{1,25},{10,2},{18... | collective-permute-start | bytes 221192 | tf_op jit(solution)/shard_map/ppermute | solution.py:18
  5.3 2.5 %collective-permute-done.1 = bf16[4,72,1,128]{3,1,2,0:T(8,128)(2,1)S(1)} collective-permute-done((bf16[4,72,1,128]{3,1,2,0:T(8,128)(2,1)S(1)}, bf16[4,72,1,128]{3,1,2,0:T(8,128)(2,1)S(1)}, u32[]{:S(2)}, u32[]{:S(2)}) %collective-permute-start.1) | collective-permute-done | bytes 73760 | tf_op jit(solution)/shard_map/ppermute | solution.py:16
  7.9 1.4 %collective-permute-done = bf16[4,72,1,128]{3,1,2,0:T(8,128)(2,1)S(1)} collective-permute-done((bf16[4,72,1,128]{3,1,2,0:T(8,128)(2,1)S(1)}, bf16[4,72,1,128]{3,1,2,0:T(8,128)(2,1)S(1)}, u32[]{:S(2)}, u32[]{:S(2)}) %collective-permute-start) | collective-permute-done | bytes 73760 | tf_op jit(solution)/shard_map/ppermute | solution.py:18
  9.3 1.1 %fusion.36 = (bf16[4,72,10,1]{3,1,2,0:T(8,128)(2,1)}, bf16[4,72,10,1]{3,1,2,0:T(8,128)(2,1)S(1)}) fusion(bf16[4,72,10,128]{3,1,2,0:T(8,128)(2,1)S(1)} %constant_dynamic-update-slice_fusion), kind=kLoop, calls=%fused_computation.97 | loop fusion | bytes 23040 | tf_op jit(solution)/shard_map/slice | solution.py:12
  10.4 1.5 %copy.29 = bf16[4,72,10,1]{1,0,3,2:T(4,128)(2,1)S(1)} copy(bf16[4,72,10,1]{3,1,2,0:T(8,128)(2,1)} %get-tuple-element.11) | data formatting | bytes 11520 | tf_op jit(solution)/shard_map/slice | solution.py:12
  11.9 2.2 %collective-permute-start.2 = (bf16[4,72,10,1]{1,0,3,2:T(4,128)(2,1)S(1)}, bf16[4,72,10,1]{1,0,3,2:T(4,128)(2,1)S(1)}, u32[]{:S(2)}, u32[]{:S(2)}) collective-permute-start(bf16[4,72,10,1]{1,0,3,2:T(4,128)(2,1)S(1)} %copy.29), channel_id=1, source_target_pairs={{1,0},{2,1},{3,2},{4,3},{5,4},{6,5},{7,6},{0,7},{9,8},{10,9},{11,1... | collective-permute-start | bytes 17288 | tf_op jit(solution)/shard_map/ppermute | solution.py:18
  14.1 0.4 copy.31
  14.9 0.6 collective-permute-done.2
  15.5 1.2 %copy.30 = bf16[4,72,10,1]{3,1,2,0:T(8,128)(2,1)} copy(bf16[4,72,10,1]{1,0,3,2:T(4,128)(2,1)S(1)} %collective-permute-done.2) | data formatting | bytes 11520 | tf_op jit(solution)/shard_map/ppermute | solution.py:18
  16.8 2.6 %collective-permute-done.3 = bf16[4,72,10,1]{1,0,3,2:T(4,128)(2,1)S(1)} collective-permute-done((bf16[4,72,10,1]{1,0,3,2:T(4,128)(2,1)S(1)}, bf16[4,72,10,1]{1,0,3,2:T(4,128)(2,1)S(1)}, u32[]{:S(2)}, u32[]{:S(2)}) %collective-permute-start.3) | collective-permute-done | bytes 5792 | tf_op jit(solution)/shard_map/ppermute | solution.py:16
  19.4 1.2 %copy.32 = bf16[4,72,10,1]{3,1,2,0:T(8,128)(2,1)} copy(bf16[4,72,10,1]{1,0,3,2:T(4,128)(2,1)S(1)} %collective-permute-done.3) | data formatting | bytes 11520 | tf_op jit(solution)/shard_map/ppermute | solution.py:16
  20.6 2.5 %fusion.5 = bf16[4,72,8,128]{3,1,2,0:T(8,128)(2,1)S(1)} fusion(bf16[4,72,8,128]{3,1,2,0:T(8,128)(2,1)S(1)} %copy.20, bf16[4,72,10,128]{3,1,2,0:T(8,128)(2,1)S(1)} %constant_dynamic-update-slice_fusion, bf16[4,72,10,1]{3,1,2,0:T(8,128)(2,1)} %copy.32, bf16[4,72,10,1]{3,1,2,0:T(8,128)(2,1)} %copy.30, bf16[4,72,1,128]{3,1,2,0:T(8,128)(2,1)S(1)} %collective-permute-done.1, ...), kind=kLoop, calls=%fused_computation.31 | loop fusion | flops 9732096 | bytes 3255552 | tf_op jit(solution)/shard_map/convert_element_type | solution.py:35
  23.1 2.2 %collective-permute-start.4 = (bf16[4,72,1,128]{3,1,2,0:T(8,128)(2,1)S(1)}, bf16[4,72,1,128]{3,1,2,0:T(8,128)(2,1)S(1)}, u32[]{:S(2)}, u32[]{:S(2)}) collective-permute-start(bf16[4,72,1,128]{3,1,2,0:T(8,128)(2,1)S(1)} %get-tuple-element.16), channel_id=1, source_target_pairs={{8,0},{16,8},{24,16},{0,24},{9,1},{17,9},{25,17},{1,25},{10,2},{18... | collective-permute-start | bytes 221192 | tf_op jit(solution)/shard_map/ppermute | solution.py:18
  25.5 1.0 %sort.17 = (s32[8]{0:T(128)}, s32[8]{0:T(128)S(1)}) sort(s32[8]{0:T(128)S(1)} %bitcast.30, s32[8]{0:T(128)S(1)} %iota.9), dimensions={0}, to_apply=%region_0.0 | sort | flops 24 | bytes 128 | tf_op jit(solution)/shard_map/jit(argsort)/sort | solution.py:47
  26.4 1.3 %collective-permute-done.4 = bf16[4,72,1,128]{3,1,2,0:T(8,128)(2,1)S(1)} collective-permute-done((bf16[4,72,1,128]{3,1,2,0:T(8,128)(2,1)S(1)}, bf16[4,72,1,128]{3,1,2,0:T(8,128)(2,1)S(1)}, u32[]{:S(2)}, u32[]{:S(2)}) %collective-permute-start.4) | collective-permute-done | bytes 73760 | tf_op jit(solution)/shard_map/ppermute | solution.py:18
  27.7 2.9 %collective-permute-done.5 = bf16[4,72,1,128]{3,1,2,0:T(8,128)(2,1)S(1)} collective-permute-done((bf16[4,72,1,128]{3,1,2,0:T(8,128)(2,1)S(1)}, bf16[4,72,1,128]{3,1,2,0:T(8,128)(2,1)S(1)}, u32[]{:S(2)}, u32[]{:S(2)}) %collective-permute-start.5) | collective-permute-done | bytes 73760 | tf_op jit(solution)/shard_map/ppermute | solution.py:16
  30.7 1.1 %fusion.35 = (bf16[4,72,10,1]{3,1,2,0:T(8,128)(2,1)}, bf16[4,72,10,1]{3,1,2,0:T(8,128)(2,1)S(1)}) fusion(bf16[4,72,10,128]{3,1,2,0:T(8,128)(2,1)S(1)} %pad_maximum_fusion), kind=kLoop, calls=%fused_computation.96 | loop fusion | bytes 23040 | tf_op jit(solution)/shard_map/slice | solution.py:12
  31.8 1.4 %copy.34 = bf16[4,72,10,1]{1,0,3,2:T(4,128)(2,1)S(1)} copy(bf16[4,72,10,1]{3,1,2,0:T(8,128)(2,1)} %get-tuple-element.9) | data formatting | bytes 11520 | tf_op jit(solution)/shard_map/slice | solution.py:12
  33.3 0.4 copy.36
  33.7 0.5 collective-permute-start.7
  34.2 0.5 collective-permute-done.6
  34.7 0.4 copy.35
  35.2 3.5 %collective-permute-done.7 = bf16[4,72,10,1]{1,0,3,2:T(4,128)(2,1)S(1)} collective-permute-done((bf16[4,72,10,1]{1,0,3,2:T(4,128)(2,1)S(1)}, bf16[4,72,10,1]{1,0,3,2:T(4,128)(2,1)S(1)}, u32[]{:S(2)}, u32[]{:S(2)}) %collective-permute-start.7) | collective-permute-done | bytes 5792 | tf_op jit(solution)/shard_map/ppermute | solution.py:16
  38.6 1.2 %copy.37 = bf16[4,72,10,1]{3,1,2,0:T(8,128)(2,1)} copy(bf16[4,72,10,1]{1,0,3,2:T(4,128)(2,1)S(1)} %collective-permute-done.7) | data formatting | bytes 11520 | tf_op jit(solution)/shard_map/ppermute | solution.py:16
  39.8 2.3 %fusion.13 = bf16[4,72,8,128]{3,1,2,0:T(8,128)(2,1)S(1)} fusion(bf16[4,72,8,128]{3,1,2,0:T(8,128)(2,1)S(1)} %fusion.5, bf16[4,72,10,1]{3,1,2,0:T(8,128)(2,1)} %copy.37, bf16[4,72,1,128]{3,1,2,0:T(8,128)(2,1)S(1)} %collective-permute-done.4, bf16[4,72,1,128]{3,1,2,0:T(8,128)(2,1)S(1)} %collective-permute-done.5, bf16[4,72,10,1]{3,1,2,0:T(8,128)(2,1)S(1)} %copy.35, ...), kind=kLoop, calls=%fused_computation.39 | loop fusion | flops 12091392 | bytes 2518272 | tf_op jit(solution)/shard_map/convert_element_type | solution.py:35
  42.2 1.2 %collective-permute-start.8 = (bf16[4,72,1,128]{3,1,2,0:T(8,128)(2,1)S(1)}, bf16[4,72,1,128]{3,1,2,0:T(8,128)(2,1)S(1)}, u32[]{:S(2)}, u32[]{:S(2)}) collective-permute-start(bf16[4,72,1,128]{3,1,2,0:T(8,128)(2,1)S(1)} %get-tuple-element.14), channel_id=1, source_target_pairs={{8,0},{16,8},{24,16},{0,24},{9,1},{17,9},{25,17},{1,25},{10,2},{18... | collective-permute-start | bytes 221192 | tf_op jit(solution)/shard_map/ppermute | solution.py:18
  43.3 0.9 %collective-permute-start.9 = (bf16[4,72,1,128]{3,1,2,0:T(8,128)(2,1)S(1)}, bf16[4,72,1,128]{3,1,2,0:T(8,128)(2,1)S(1)}, u32[]{:S(2)}, u32[]{:S(2)}) collective-permute-start(bf16[4,72,1,128]{3,1,2,0:T(8,128)(2,1)S(1)} %get-tuple-element.13), channel_id=1, source_target_pairs={{0,8},{8,16},{16,24},{24,0},{1,9},{9,17},{17,25},{25,1},{2,10},{10... | collective-permute-start | bytes 221192 | tf_op jit(solution)/shard_map/ppermute | solution.py:16
  44.2 2.3 %collective-permute-done.8 = bf16[4,72,1,128]{3,1,2,0:T(8,128)(2,1)S(1)} collective-permute-done((bf16[4,72,1,128]{3,1,2,0:T(8,128)(2,1)S(1)}, bf16[4,72,1,128]{3,1,2,0:T(8,128)(2,1)S(1)}, u32[]{:S(2)}, u32[]{:S(2)}) %collective-permute-start.8) | collective-permute-done | bytes 73760 | tf_op jit(solution)/shard_map/ppermute | solution.py:18
  46.6 2.0 %collective-permute-done.9 = bf16[4,72,1,128]{3,1,2,0:T(8,128)(2,1)S(1)} collective-permute-done((bf16[4,72,1,128]{3,1,2,0:T(8,128)(2,1)S(1)}, bf16[4,72,1,128]{3,1,2,0:T(8,128)(2,1)S(1)}, u32[]{:S(2)}, u32[]{:S(2)}) %collective-permute-start.9) | collective-permute-done | bytes 73760 | tf_op jit(solution)/shard_map/ppermute | solution.py:16
  48.7 0.3 fusion.34
  49.0 0.4 copy.38
  49.3 0.4 copy.40
  49.7 0.5 collective-permute-start.11
  50.2 0.5 collective-permute-done.10
  50.7 0.4 copy.39
  51.2 3.5 %collective-permute-done.11 = bf16[4,72,10,1]{1,0,3,2:T(4,128)(2,1)S(1)} collective-permute-done((bf16[4,72,10,1]{1,0,3,2:T(4,128)(2,1)S(1)}, bf16[4,72,10,1]{1,0,3,2:T(4,128)(2,1)S(1)}, u32[]{:S(2)}, u32[]{:S(2)}) %collective-permute-start.11) | collective-permute-done | bytes 5792 | tf_op jit(solution)/shard_map/ppermute | solution.py:16
  54.6 0.4 copy.41
  55.1 2.0 %fusion.21 = bf16[4,72,8,128]{3,1,2,0:T(8,128)(2,1)} fusion(bf16[4,72,8,128]{3,1,2,0:T(8,128)(2,1)S(1)} %fusion.13, bf16[4,72,10,1]{3,1,2,0:T(8,128)(2,1)S(1)} %copy.41, bf16[4,72,1,128]{3,1,2,0:T(8,128)(2,1)S(1)} %collective-permute-done.8, bf16[4,72,1,128]{3,1,2,0:T(8,128)(2,1)S(1)} %collective-permute-done.9, bf16[4,72,10,1]{3,1,2,0:T(8,128)(2,1)S(1)} %copy.39, ...), kind=kLoop, calls=%fused_computation.47 | loop fusion | flops 12091392 | bytes 2518272 | tf_op jit(solution)/shard_map/convert_element_type | solution.py:35
  57.1 1.7 %gather_fusion = bf16[8,4,72,128]{3,2,1,0:T(8,128)(2,1)S(1)} fusion(bf16[4,72,8,128]{3,1,2,0:T(8,128)(2,1)} %fusion.21, s32[1024]{0:T(1024)S(1)} %pad_clamp_fusion), kind=kCustom, calls=%fused_computation | custom fusion | bytes 1179680 | tf_op jit(solution)/shard_map/jit(_take)/gather | solution.py:49
  58.9 0.9 %select_bitcast_fusion = bf16[4,72,8,128]{3,1,0,2:T(8,128)(2,1)} fusion(bf16[8,4,72,128]{3,2,1,0:T(8,128)(2,1)S(1)} %gather_fusion, pred[8]{0:T(512)(128)(4,1)S(1)} %compare_and_fusion), kind=kLoop, calls=%fused_computation.77 | loop fusion | flops 294912 | bytes 1179656 | tf_op jit(solution)/shard_map/jit(_take)/select_n | solution.py:49
  59.8 3.5 %all-to-all-start = ((bf16[4,72,8,128]{3,1,0,2:T(8,128)(2,1)}), bf16[4,72,8,128]{3,1,0,2:T(8,128)(2,1)S(1)}, u32[]{:S(2)}, u32[]{:S(2)}) async-start(bf16[4,72,8,128]{3,1,0,2:T(8,128)(2,1)} %select_bitcast_fusion), calls=%async_computation | async-start | bytes 1179648 | tf_op jit(solution)/shard_map/all_to_all | solution.py:50
  64.0 0.1 select_reduce_fusion
  64.2 15.9 %all-to-all-done = bf16[4,72,8,128]{3,1,0,2:T(8,128)(2,1)S(1)} async-done(((bf16[4,72,8,128]{3,1,0,2:T(8,128)(2,1)}), bf16[4,72,8,128]{3,1,0,2:T(8,128)(2,1)S(1)}, u32[]{:S(2)}, u32[]{:S(2)}) %all-to-all-start) | async-done | bytes 589856 | tf_op jit(solution)/shard_map/all_to_all | solution.py:50
  80.0 0.3 fusion.27
  80.3 0.3 fusion.1
  80.6 0.9 %copy.43 = bf16[4,72,8,128]{3,2,1,0:T(8,128)(2,1)} copy(bf16[4,72,8,128]{3,1,2,0:T(8,128)(2,1)S(1)} %fusion.1) | data formatting | bytes 1179648 | tf_op jit(solution)/shard_map/convert_element_type | solution.py:57
  (32 shorter events, 1.0 us)
Async XLA Ops:
  0.0 80.0 %copy-start = (bf16[1,72,72]{2,1,0:T(8,128)(2,1)S(1)}, bf16[1,72,72]{2,1,0:T(8,128)(2,1)}, u32[]{:S(2)}) copy-start(bf16[1,72,72]{2,1,0:T(8,128)(2,1)} %param.9) | copy-start | bytes 31108
  0.0 7.8 %copy-start.1 = (bf16[4,72,8,128]{3,2,1,0:T(8,128)(2,1)S(1)}, bf16[4,72,8,128]{3,2,1,0:T(8,128)(2,1)}, u32[]{:S(2)}) copy-start(bf16[4,72,8,128]{3,2,1,0:T(8,128)(2,1)} %param.6) | copy-start | bytes 1769476
  1.2 6.5 %collective-permute-start.1 = (bf16[4,72,1,128]{3,1,2,0:T(8,128)(2,1)S(1)}, bf16[4,72,1,128]{3,1,2,0:T(8,128)(2,1)S(1)}, u32[]{:S(2)}, u32[]{:S(2)}) collective-permute-start(bf16[4,72,1,128]{3,1,2,0:T(8,128)(2,1)S(1)} %get-tuple-element.18), channel_id=1, source_target_pairs={{0,8},{8,16},{16,24},{24,0},{1,9},{9,17},{17,25},{25,1},{2,10},{10... | collective-permute-start | bytes 221192 | tf_op jit(solution)/shard_map/ppermute | solution.py:16
  4.2 5.1 %collective-permute-start = (bf16[4,72,1,128]{3,1,2,0:T(8,128)(2,1)S(1)}, bf16[4,72,1,128]{3,1,2,0:T(8,128)(2,1)S(1)}, u32[]{:S(2)}, u32[]{:S(2)}) collective-permute-start(bf16[4,72,1,128]{3,1,2,0:T(8,128)(2,1)S(1)} %get-tuple-element.17), channel_id=1, source_target_pairs={{8,0},{16,8},{24,16},{0,24},{9,1},{17,9},{25,17},{1,25},{10,2},{18... | collective-permute-start | bytes 221192 | tf_op jit(solution)/shard_map/ppermute | solution.py:18
  10.4 4.1 %copy-start.3 = (bf16[2,72,8,128]{3,2,1,0:T(8,128)(2,1)S(1)}, bf16[2,72,8,128]{3,2,1,0:T(8,128)(2,1)}, u32[]{:S(2)}) copy-start(bf16[2,72,8,128]{3,2,1,0:T(8,128)(2,1)} %param.7) | copy-start | bytes 884740
  11.9 3.6 %collective-permute-start.2 = (bf16[4,72,10,1]{1,0,3,2:T(4,128)(2,1)S(1)}, bf16[4,72,10,1]{1,0,3,2:T(4,128)(2,1)S(1)}, u32[]{:S(2)}, u32[]{:S(2)}) collective-permute-start(bf16[4,72,10,1]{1,0,3,2:T(4,128)(2,1)S(1)} %copy.29), channel_id=1, source_target_pairs={{1,0},{2,1},{3,2},{4,3},{5,4},{6,5},{7,6},{0,7},{9,8},{10,9},{11,1... | collective-permute-start | bytes 17288 | tf_op jit(solution)/shard_map/ppermute | solution.py:18
  14.5 4.9 %collective-permute-start.3 = (bf16[4,72,10,1]{1,0,3,2:T(4,128)(2,1)S(1)}, bf16[4,72,10,1]{1,0,3,2:T(4,128)(2,1)S(1)}, u32[]{:S(2)}, u32[]{:S(2)}) collective-permute-start(bf16[4,72,10,1]{1,0,3,2:T(4,128)(2,1)S(1)} %copy.31), channel_id=1, source_target_pairs={{0,1},{1,2},{2,3},{3,4},{4,5},{5,6},{6,7},{7,0},{8,9},{9,10},{10,1... | collective-permute-start | bytes 17288 | tf_op jit(solution)/shard_map/ppermute | solution.py:16
  20.6 4.8 %copy-start.4 = (s32[1,8]{1,0:T(1,128)S(1)}, s32[1,8]{1,0:T(1,128)}, u32[]{:S(2)}) copy-start(s32[1,8]{1,0:T(1,128)} %param.8) | copy-start | bytes 100
  23.1 4.6 %collective-permute-start.4 = (bf16[4,72,1,128]{3,1,2,0:T(8,128)(2,1)S(1)}, bf16[4,72,1,128]{3,1,2,0:T(8,128)(2,1)S(1)}, u32[]{:S(2)}, u32[]{:S(2)}) collective-permute-start(bf16[4,72,1,128]{3,1,2,0:T(8,128)(2,1)S(1)} %get-tuple-element.16), channel_id=1, source_target_pairs={{8,0},{16,8},{24,16},{0,24},{9,1},{17,9},{25,17},{1,25},{10,2},{18... | collective-permute-start | bytes 221192 | tf_op jit(solution)/shard_map/ppermute | solution.py:18
  25.4 5.3 %collective-permute-start.5 = (bf16[4,72,1,128]{3,1,2,0:T(8,128)(2,1)S(1)}, bf16[4,72,1,128]{3,1,2,0:T(8,128)(2,1)S(1)}, u32[]{:S(2)}, u32[]{:S(2)}) collective-permute-start(bf16[4,72,1,128]{3,1,2,0:T(8,128)(2,1)S(1)} %get-tuple-element.15), channel_id=1, source_target_pairs={{0,8},{8,16},{16,24},{24,0},{1,9},{9,17},{17,25},{25,1},{2,10},{10... | collective-permute-start | bytes 221192 | tf_op jit(solution)/shard_map/ppermute | solution.py:16
  33.3 1.4 %collective-permute-start.6 = (bf16[4,72,10,1]{1,0,3,2:T(4,128)(2,1)S(1)}, bf16[4,72,10,1]{1,0,3,2:T(4,128)(2,1)S(1)}, u32[]{:S(2)}, u32[]{:S(2)}) collective-permute-start(bf16[4,72,10,1]{1,0,3,2:T(4,128)(2,1)S(1)} %copy.34), channel_id=1, source_target_pairs={{1,0},{2,1},{3,2},{4,3},{5,4},{6,5},{7,6},{0,7},{9,8},{10,9},{11,1... | collective-permute-start | bytes 17288 | tf_op jit(solution)/shard_map/ppermute | solution.py:18
  33.7 4.9 %collective-permute-start.7 = (bf16[4,72,10,1]{1,0,3,2:T(4,128)(2,1)S(1)}, bf16[4,72,10,1]{1,0,3,2:T(4,128)(2,1)S(1)}, u32[]{:S(2)}, u32[]{:S(2)}) collective-permute-start(bf16[4,72,10,1]{1,0,3,2:T(4,128)(2,1)S(1)} %copy.36), channel_id=1, source_target_pairs={{0,1},{1,2},{2,3},{3,4},{4,5},{5,6},{6,7},{7,0},{8,9},{9,10},{10,1... | collective-permute-start | bytes 17288 | tf_op jit(solution)/shard_map/ppermute | solution.py:16
  42.2 4.4 %collective-permute-start.8 = (bf16[4,72,1,128]{3,1,2,0:T(8,128)(2,1)S(1)}, bf16[4,72,1,128]{3,1,2,0:T(8,128)(2,1)S(1)}, u32[]{:S(2)}, u32[]{:S(2)}) collective-permute-start(bf16[4,72,1,128]{3,1,2,0:T(8,128)(2,1)S(1)} %get-tuple-element.14), channel_id=1, source_target_pairs={{8,0},{16,8},{24,16},{0,24},{9,1},{17,9},{25,17},{1,25},{10,2},{18... | collective-permute-start | bytes 221192 | tf_op jit(solution)/shard_map/ppermute | solution.py:18
  43.3 5.3 %collective-permute-start.9 = (bf16[4,72,1,128]{3,1,2,0:T(8,128)(2,1)S(1)}, bf16[4,72,1,128]{3,1,2,0:T(8,128)(2,1)S(1)}, u32[]{:S(2)}, u32[]{:S(2)}) collective-permute-start(bf16[4,72,1,128]{3,1,2,0:T(8,128)(2,1)S(1)} %get-tuple-element.13), channel_id=1, source_target_pairs={{0,8},{8,16},{16,24},{24,0},{1,9},{9,17},{17,25},{25,1},{2,10},{10... | collective-permute-start | bytes 221192 | tf_op jit(solution)/shard_map/ppermute | solution.py:16
  49.3 1.4 %collective-permute-start.10 = (bf16[4,72,10,1]{1,0,3,2:T(4,128)(2,1)S(1)}, bf16[4,72,10,1]{1,0,3,2:T(4,128)(2,1)S(1)}, u32[]{:S(2)}, u32[]{:S(2)}) collective-permute-start(bf16[4,72,10,1]{1,0,3,2:T(4,128)(2,1)S(1)} %copy.38), channel_id=1, source_target_pairs={{1,0},{2,1},{3,2},{4,3},{5,4},{6,5},{7,6},{0,7},{9,8},{10,9},{11,1... | collective-permute-start | bytes 17288 | tf_op jit(solution)/shard_map/ppermute | solution.py:18
  49.7 4.9 %collective-permute-start.11 = (bf16[4,72,10,1]{1,0,3,2:T(4,128)(2,1)S(1)}, bf16[4,72,10,1]{1,0,3,2:T(4,128)(2,1)S(1)}, u32[]{:S(2)}, u32[]{:S(2)}) collective-permute-start(bf16[4,72,10,1]{1,0,3,2:T(4,128)(2,1)S(1)} %copy.40), channel_id=1, source_target_pairs={{0,1},{1,2},{2,3},{3,4},{4,5},{5,6},{6,7},{7,0},{8,9},{9,10},{10,1... | collective-permute-start | bytes 17288 | tf_op jit(solution)/shard_map/ppermute | solution.py:16
  58.8 5.2 %copy-start.2 = (bf16[16,72,72]{2,1,0:T(8,128)(2,1)S(1)}, bf16[16,72,72]{2,1,0:T(8,128)(2,1)}, u32[]{:S(2)}) copy-start(bf16[16,72,72]{2,1,0:T(8,128)(2,1)} %param.11) | copy-start | bytes 497668
  59.8 20.2 %all-to-all-start = ((bf16[4,72,8,128]{3,1,0,2:T(8,128)(2,1)}), bf16[4,72,8,128]{3,1,0,2:T(8,128)(2,1)S(1)}, u32[]{:S(2)}, u32[]{:S(2)}) async-start(bf16[4,72,8,128]{3,1,0,2:T(8,128)(2,1)} %select_bitcast_fusion), calls=%async_computation | async-start | bytes 1179648 | tf_op jit(solution)/shard_map/all_to_all | solution.py:50
where the time goes:
time: 81.9 us; the launch traced here: 81.5 us
  waiting for transfers between devices  39.4 us (48%)
  local copies, waits for them, and re-layouts  16.2 us (20%)
  starting transfers between devices  15.3 us (19%)
  other arithmetic  9.14 us (11%)
  between operations  0.86 us (1%)
    ppermute x6, waiting for transfers between devices, with_halo(): lax.ppermute(tail, axis, [(i, (i + 1) % count) for i in range(count)])  16.9 us
    all_to_all x1, waiting for transfers between devices, per_device(): lax.all_to_all(ordered, 'tile', split_axis=2, concat_axis=2, tiled=True)  15.9 us
    convert_element_type x3, other arithmetic, advect_tile(): return out.astype(jnp.bfloat16)  6.8 us
    ppermute x6, starting transfers between devices, with_halo(): lax.ppermute(head, axis, [((i + 1) % count, i) for i in range(count)])  6.67 us
    ppermute x6, waiting for transfers between devices, with_halo(): lax.ppermute(head, axis, [((i + 1) % count, i) for i in range(count)])  6.61 us
    slice x7, local copies, waits for them, and re-layouts, with_halo(): head = lax.slice_in_dim(cells, 0, width, axis=dim)  5.84 us
    ppermute x6, starting transfers between devices, with_halo(): lax.ppermute(tail, axis, [(i, (i + 1) % count) for i in range(count)])  5.11 us
    all_to_all x1, starting transfers between devices, per_device(): lax.all_to_all(ordered, 'tile', split_axis=2, concat_axis=2, tiled=True)  3.54 us
  transfers between devices with their start and end apart: 13, of which 13 were waited for; matrix products, arithmetic and copies ran while one was open for 6% of the time, Pallas kernels for 0%

commit v1 on v0

--- a/solution.py
+++ b/solution.py
@@ -47,7 +47,10 @@
     order = jnp.argsort(destination[0])
     band_count = band_table.shape[0]
     ordered = jnp.take(advected, order, axis=2)
-    received = lax.all_to_all(ordered, "tile", split_axis=2, concat_axis=2, tiled=True)
+    received = jnp.concatenate(
+        lax.all_to_all(jnp.stack(jnp.split(ordered, lax.axis_size("tile"), axis=2)), "tile", 0, 0),
+        axis=2,
+    )
     inverse = diffusion[0]
     diffused = jnp.einsum("kl,tlxy->tkxy", inverse, received, preferred_element_type=jnp.float32)
     diffused16 = diffused.astype(jnp.bfloat16)

time: 81.9 us -> 86.2 us (1.053)
  local copies, waits for them, and re-layouts: 16.2 us -> 21.3 us
    unnamed x13 -> x20, local copies, waits for them, and re-layouts: 1.37 us -> 5.84 us
where the time goes in v1:
time: 86.2 us; the launch traced here: 85.8 us
  waiting for transfers between devices  39.4 us (46%)
  local copies, waits for them, and re-layouts  21.3 us (25%)
  starting transfers between devices  15.3 us (18%)
  other arithmetic  8.33 us (10%)
  between operations  0.87 us (1%)
    ppermute x6, waiting for transfers between devices, with_halo(): lax.ppermute(tail, axis, [(i, (i + 1) % count) for i in range(count)])  16.9 us
    all_to_all x1, waiting for transfers between devices, per_device(): lax.all_to_all(jnp.stack(jnp.split(ordered, lax.axis_size('tile'), axis=2...  15.9 us
    convert_element_type x3, other arithmetic, advect_tile(): return out.astype(jnp.bfloat16)  6.8 us
    ppermute x6, starting transfers between devices, with_halo(): lax.ppermute(head, axis, [((i + 1) % count, i) for i in range(count)])  6.67 us
    ppermute x6, waiting for transfers between devices, with_halo(): lax.ppermute(head, axis, [((i + 1) % count, i) for i in range(count)])  6.6 us
    slice x7, local copies, waits for them, and re-layouts, with_halo(): head = lax.slice_in_dim(cells, 0, width, axis=dim)  5.84 us
    unnamed x20, local copies, waits for them, and re-layouts  5.84 us
    ppermute x6, starting transfers between devices, with_halo(): lax.ppermute(tail, axis, [(i, (i + 1) % count) for i in range(count)])  5.11 us
  transfers between devices with their start and end apart: 13, of which 13 were waited for; matrix products, arithmetic and copies ran while one was open for 6% of the time, Pallas kernels for 0%

profile of v1, /device:TPU:0, one launch (start us, length us, event | category | flops | bytes accessed | tf_op | source)
XLA Modules:
  0.0 85.8 jit_solution(786491054482240294)
XLA Ops:
  0.0 1.2 %copy.33 = bf16[4,72,8,128]{3,1,2,0:T(8,128)(2,1)S(1)} copy(bf16[4,72,8,128]{3,2,1,0:T(8,128)(2,1)} %param.6) | data formatting | bytes 1179648 | tf_op args[0]
  1.2 3.0 %collective-permute-start.1 = (bf16[4,72,1,128]{3,1,2,0:T(8,128)(2,1)S(1)}, bf16[4,72,1,128]{3,1,2,0:T(8,128)(2,1)S(1)}, u32[]{:S(2)}, u32[]{:S(2)}) collective-permute-start(bf16[4,72,1,128]{3,1,2,0:T(8,128)(2,1)S(1)} %get-tuple-element.18), channel_id=1, source_target_pairs={{0,8},{8,16},{16,24},{24,0},{1,9},{9,17},{17,25},{25,1},{2,10},{10... | collective-permute-start | bytes 221192 | tf_op jit(solution)/shard_map/ppermute | solution.py:16
  4.2 1.0 %collective-permute-start = (bf16[4,72,1,128]{3,1,2,0:T(8,128)(2,1)S(1)}, bf16[4,72,1,128]{3,1,2,0:T(8,128)(2,1)S(1)}, u32[]{:S(2)}, u32[]{:S(2)}) collective-permute-start(bf16[4,72,1,128]{3,1,2,0:T(8,128)(2,1)S(1)} %get-tuple-element.17), channel_id=1, source_target_pairs={{8,0},{16,8},{24,16},{0,24},{9,1},{17,9},{25,17},{1,25},{10,2},{18... | collective-permute-start | bytes 221192 | tf_op jit(solution)/shard_map/ppermute | solution.py:18
  5.3 2.5 %collective-permute-done.1 = bf16[4,72,1,128]{3,1,2,0:T(8,128)(2,1)S(1)} collective-permute-done((bf16[4,72,1,128]{3,1,2,0:T(8,128)(2,1)S(1)}, bf16[4,72,1,128]{3,1,2,0:T(8,128)(2,1)S(1)}, u32[]{:S(2)}, u32[]{:S(2)}) %collective-permute-start.1) | collective-permute-done | bytes 73760 | tf_op jit(solution)/shard_map/ppermute | solution.py:16
  7.9 1.4 %collective-permute-done = bf16[4,72,1,128]{3,1,2,0:T(8,128)(2,1)S(1)} collective-permute-done((bf16[4,72,1,128]{3,1,2,0:T(8,128)(2,1)S(1)}, bf16[4,72,1,128]{3,1,2,0:T(8,128)(2,1)S(1)}, u32[]{:S(2)}, u32[]{:S(2)}) %collective-permute-start) | collective-permute-done | bytes 73760 | tf_op jit(solution)/shard_map/ppermute | solution.py:18
  9.3 1.1 %fusion.45 = (bf16[4,72,10,1]{3,1,2,0:T(8,128)(2,1)}, bf16[4,72,10,1]{3,1,2,0:T(8,128)(2,1)S(1)}) fusion(bf16[4,72,10,128]{3,1,2,0:T(8,128)(2,1)S(1)} %constant_dynamic-update-slice_fusion), kind=kLoop, calls=%fused_computation.114 | loop fusion | bytes 23040 | tf_op jit(solution)/shard_map/slice | solution.py:12
  10.4 1.5 %copy.42 = bf16[4,72,10,1]{1,0,3,2:T(4,128)(2,1)S(1)} copy(bf16[4,72,10,1]{3,1,2,0:T(8,128)(2,1)} %get-tuple-element.11) | data formatting | bytes 11520 | tf_op jit(solution)/shard_map/slice | solution.py:12
  11.9 2.2 %collective-permute-start.2 = (bf16[4,72,10,1]{1,0,3,2:T(4,128)(2,1)S(1)}, bf16[4,72,10,1]{1,0,3,2:T(4,128)(2,1)S(1)}, u32[]{:S(2)}, u32[]{:S(2)}) collective-permute-start(bf16[4,72,10,1]{1,0,3,2:T(4,128)(2,1)S(1)} %copy.42), channel_id=1, source_target_pairs={{1,0},{2,1},{3,2},{4,3},{5,4},{6,5},{7,6},{0,7},{9,8},{10,9},{11,1... | collective-permute-start | bytes 17288 | tf_op jit(solution)/shard_map/ppermute | solution.py:18
  14.9 0.6 collective-permute-done.2
  15.5 1.2 %copy.43 = bf16[4,72,10,1]{3,1,2,0:T(8,128)(2,1)} copy(bf16[4,72,10,1]{1,0,3,2:T(4,128)(2,1)S(1)} %collective-permute-done.2) | data formatting | bytes 11520 | tf_op jit(solution)/shard_map/ppermute | solution.py:18
  16.8 2.6 %collective-permute-done.3 = bf16[4,72,10,1]{1,0,3,2:T(4,128)(2,1)S(1)} collective-permute-done((bf16[4,72,10,1]{1,0,3,2:T(4,128)(2,1)S(1)}, bf16[4,72,10,1]{1,0,3,2:T(4,128)(2,1)S(1)}, u32[]{:S(2)}, u32[]{:S(2)}) %collective-permute-start.3) | collective-permute-done | bytes 5792 | tf_op jit(solution)/shard_map/ppermute | solution.py:16
  19.4 1.2 %copy.45 = bf16[4,72,10,1]{3,1,2,0:T(8,128)(2,1)} copy(bf16[4,72,10,1]{1,0,3,2:T(4,128)(2,1)S(1)} %collective-permute-done.3) | data formatting | bytes 11520 | tf_op jit(solution)/shard_map/ppermute | solution.py:16
  20.6 2.5 %fusion.5 = bf16[4,72,8,128]{3,1,2,0:T(8,128)(2,1)S(1)} fusion(bf16[4,72,8,128]{3,1,2,0:T(8,128)(2,1)S(1)} %copy.33, bf16[4,72,10,128]{3,1,2,0:T(8,128)(2,1)S(1)} %constant_dynamic-update-slice_fusion, bf16[4,72,10,1]{3,1,2,0:T(8,128)(2,1)} %copy.45, bf16[4,72,10,1]{3,1,2,0:T(8,128)(2,1)} %copy.43, bf16[4,72,1,128]{3,1,2,0:T(8,128)(2,1)S(1)} %collective-permute-done.1, ...), kind=kLoop, calls=%fused_computation.31 | loop fusion | flops 9732096 | bytes 3255552 | tf_op jit(solution)/shard_map/convert_element_type | solution.py:35
  23.1 2.2 %collective-permute-start.4 = (bf16[4,72,1,128]{3,1,2,0:T(8,128)(2,1)S(1)}, bf16[4,72,1,128]{3,1,2,0:T(8,128)(2,1)S(1)}, u32[]{:S(2)}, u32[]{:S(2)}) collective-permute-start(bf16[4,72,1,128]{3,1,2,0:T(8,128)(2,1)S(1)} %get-tuple-element.16), channel_id=1, source_target_pairs={{8,0},{16,8},{24,16},{0,24},{9,1},{17,9},{25,17},{1,25},{10,2},{18... | collective-permute-start | bytes 221192 | tf_op jit(solution)/shard_map/ppermute | solution.py:18
  25.5 1.0 %sort.17 = (s32[8]{0:T(128)}, s32[8]{0:T(128)S(1)}) sort(s32[8]{0:T(128)S(1)} %bitcast.67, s32[8]{0:T(128)S(1)} %iota.9), dimensions={0}, to_apply=%region_0.0 | sort | flops 24 | bytes 128 | tf_op jit(solution)/shard_map/jit(argsort)/sort | solution.py:47
  26.4 1.3 %collective-permute-done.4 = bf16[4,72,1,128]{3,1,2,0:T(8,128)(2,1)S(1)} collective-permute-done((bf16[4,72,1,128]{3,1,2,0:T(8,128)(2,1)S(1)}, bf16[4,72,1,128]{3,1,2,0:T(8,128)(2,1)S(1)}, u32[]{:S(2)}, u32[]{:S(2)}) %collective-permute-start.4) | collective-permute-done | bytes 73760 | tf_op jit(solution)/shard_map/ppermute | solution.py:18
  27.7 2.9 %collective-permute-done.5 = bf16[4,72,1,128]{3,1,2,0:T(8,128)(2,1)S(1)} collective-permute-done((bf16[4,72,1,128]{3,1,2,0:T(8,128)(2,1)S(1)}, bf16[4,72,1,128]{3,1,2,0:T(8,128)(2,1)S(1)}, u32[]{:S(2)}, u32[]{:S(2)}) %collective-permute-start.5) | collective-permute-done | bytes 73760 | tf_op jit(solution)/shard_map/ppermute | solution.py:16
  30.7 1.1 %fusion.44 = (bf16[4,72,10,1]{3,1,2,0:T(8,128)(2,1)}, bf16[4,72,10,1]{3,1,2,0:T(8,128)(2,1)S(1)}) fusion(bf16[4,72,10,128]{3,1,2,0:T(8,128)(2,1)S(1)} %pad_maximum_fusion), kind=kLoop, calls=%fused_computation.113 | loop fusion | bytes 23040 | tf_op jit(solution)/shard_map/slice | solution.py:12
  31.8 1.4 %copy.47 = bf16[4,72,10,1]{1,0,3,2:T(4,128)(2,1)S(1)} copy(bf16[4,72,10,1]{3,1,2,0:T(8,128)(2,1)} %get-tuple-element.9) | data formatting | bytes 11520 | tf_op jit(solution)/shard_map/slice | solution.py:12
  33.7 0.5 collective-permute-start.7
  34.2 0.5 collective-permute-done.6
  34.7 0.4 copy.48
  35.2 3.5 %collective-permute-done.7 = bf16[4,72,10,1]{1,0,3,2:T(4,128)(2,1)S(1)} collective-permute-done((bf16[4,72,10,1]{1,0,3,2:T(4,128)(2,1)S(1)}, bf16[4,72,10,1]{1,0,3,2:T(4,128)(2,1)S(1)}, u32[]{:S(2)}, u32[]{:S(2)}) %collective-permute-start.7) | collective-permute-done | bytes 5792 | tf_op jit(solution)/shard_map/ppermute | solution.py:16
  38.6 1.2 %copy.50 = bf16[4,72,10,1]{3,1,2,0:T(8,128)(2,1)} copy(bf16[4,72,10,1]{1,0,3,2:T(4,128)(2,1)S(1)} %collective-permute-done.7) | data formatting | bytes 11520 | tf_op jit(solution)/shard_map/ppermute | solution.py:16
  39.8 2.3 %fusion.13 = bf16[4,72,8,128]{3,1,2,0:T(8,128)(2,1)S(1)} fusion(bf16[4,72,8,128]{3,1,2,0:T(8,128)(2,1)S(1)} %fusion.5, bf16[4,72,10,1]{3,1,2,0:T(8,128)(2,1)} %copy.50, bf16[4,72,1,128]{3,1,2,0:T(8,128)(2,1)S(1)} %collective-permute-done.4, bf16[4,72,1,128]{3,1,2,0:T(8,128)(2,1)S(1)} %collective-permute-done.5, bf16[4,72,10,1]{3,1,2,0:T(8,128)(2,1)S(1)} %copy.48, ...), kind=kLoop, calls=%fused_computation.39 | loop fusion | flops 12091392 | bytes 2518272 | tf_op jit(solution)/shard_map/convert_element_type | solution.py:35
  42.2 1.2 %collective-permute-start.8 = (bf16[4,72,1,128]{3,1,2,0:T(8,128)(2,1)S(1)}, bf16[4,72,1,128]{3,1,2,0:T(8,128)(2,1)S(1)}, u32[]{:S(2)}, u32[]{:S(2)}) collective-permute-start(bf16[4,72,1,128]{3,1,2,0:T(8,128)(2,1)S(1)} %get-tuple-element.14), channel_id=1, source_target_pairs={{8,0},{16,8},{24,16},{0,24},{9,1},{17,9},{25,17},{1,25},{10,2},{18... | collective-permute-start | bytes 221192 | tf_op jit(solution)/shard_map/ppermute | solution.py:18
  43.3 0.9 %collective-permute-start.9 = (bf16[4,72,1,128]{3,1,2,0:T(8,128)(2,1)S(1)}, bf16[4,72,1,128]{3,1,2,0:T(8,128)(2,1)S(1)}, u32[]{:S(2)}, u32[]{:S(2)}) collective-permute-start(bf16[4,72,1,128]{3,1,2,0:T(8,128)(2,1)S(1)} %get-tuple-element.13), channel_id=1, source_target_pairs={{0,8},{8,16},{16,24},{24,0},{1,9},{9,17},{17,25},{25,1},{2,10},{10... | collective-permute-start | bytes 221192 | tf_op jit(solution)/shard_map/ppermute | solution.py:16
  44.2 2.3 %collective-permute-done.8 = bf16[4,72,1,128]{3,1,2,0:T(8,128)(2,1)S(1)} collective-permute-done((bf16[4,72,1,128]{3,1,2,0:T(8,128)(2,1)S(1)}, bf16[4,72,1,128]{3,1,2,0:T(8,128)(2,1)S(1)}, u32[]{:S(2)}, u32[]{:S(2)}) %collective-permute-start.8) | collective-permute-done | bytes 73760 | tf_op jit(solution)/shard_map/ppermute | solution.py:18
  46.6 2.0 %collective-permute-done.9 = bf16[4,72,1,128]{3,1,2,0:T(8,128)(2,1)S(1)} collective-permute-done((bf16[4,72,1,128]{3,1,2,0:T(8,128)(2,1)S(1)}, bf16[4,72,1,128]{3,1,2,0:T(8,128)(2,1)S(1)}, u32[]{:S(2)}, u32[]{:S(2)}) %collective-permute-start.9) | collective-permute-done | bytes 73760 | tf_op jit(solution)/shard_map/ppermute | solution.py:16
  49.0 0.4 copy.51
  49.7 0.5 collective-permute-start.11
  50.2 0.5 collective-permute-done.10
  50.7 0.4 copy.52
  51.2 3.5 %collective-permute-done.11 = bf16[4,72,10,1]{1,0,3,2:T(4,128)(2,1)S(1)} collective-permute-done((bf16[4,72,10,1]{1,0,3,2:T(4,128)(2,1)S(1)}, bf16[4,72,10,1]{1,0,3,2:T(4,128)(2,1)S(1)}, u32[]{:S(2)}, u32[]{:S(2)}) %collective-permute-start.11) | collective-permute-done | bytes 5792 | tf_op jit(solution)/shard_map/ppermute | solution.py:16
  54.6 0.4 copy.54
  55.1 2.0 %fusion.21 = bf16[4,72,8,128]{3,1,2,0:T(8,128)(2,1)} fusion(bf16[4,72,8,128]{3,1,2,0:T(8,128)(2,1)S(1)} %fusion.13, bf16[4,72,10,1]{3,1,2,0:T(8,128)(2,1)S(1)} %copy.54, bf16[4,72,1,128]{3,1,2,0:T(8,128)(2,1)S(1)} %collective-permute-done.8, bf16[4,72,1,128]{3,1,2,0:T(8,128)(2,1)S(1)} %collective-permute-done.9, bf16[4,72,10,1]{3,1,2,0:T(8,128)(2,1)S(1)} %copy.52, ...), kind=kLoop, calls=%fused_computation.47 | loop fusion | flops 12091392 | bytes 2518272 | tf_op jit(solution)/shard_map/convert_element_type | solution.py:35
  57.1 1.7 %gather_fusion = bf16[8,4,72,128]{3,2,1,0:T(8,128)(2,1)S(1)} fusion(bf16[4,72,8,128]{3,1,2,0:T(8,128)(2,1)} %fusion.21, s32[1024]{0:T(1024)S(1)} %pad_clamp_fusion), kind=kCustom, calls=%fused_computation | custom fusion | bytes 1179680 | tf_op jit(solution)/shard_map/jit(_take)/gather | solution.py:49
  59.0 0.6 fusion.40
  59.6 0.6 fusion.39
  60.3 0.6 fusion.38
  60.9 0.6 fusion.37
  61.5 0.6 fusion.36
  62.2 0.6 fusion.35
  62.8 0.6 fusion.34
  63.5 0.6 fusion.33
  64.1 3.5 %all-to-all-start = ((bf16[8,4,72,1,128]{4,2,1,3,0:T(8,128)(2,1)}), bf16[8,4,72,1,128]{4,2,1,3,0:T(8,128)(2,1)S(1)}, u32[]{:S(2)}, u32[]{:S(2)}) async-start(bf16[8,4,72,1,128]{4,2,1,3,0:T(8,128)(2,1)} %fusion.33), calls=%async_computation | async-start | bytes 1179648 | tf_op jit(solution)/shard_map/all_to_all | solution.py:51
  68.5 15.9 %all-to-all-done = bf16[8,4,72,1,128]{4,2,1,3,0:T(8,128)(2,1)S(1)} async-done(((bf16[8,4,72,1,128]{4,2,1,3,0:T(8,128)(2,1)}), bf16[8,4,72,1,128]{4,2,1,3,0:T(8,128)(2,1)S(1)}, u32[]{:S(2)}, u32[]{:S(2)}) %all-to-all-start) | async-done | bytes 589856 | tf_op jit(solution)/shard_map/all_to_all | solution.py:51
  84.9 0.9 %copy.56 = bf16[4,72,8,128]{3,2,1,0:T(8,128)(2,1)} copy(bf16[4,72,8,128]{3,1,2,0:T(8,128)(2,1)S(1)} %fusion.1) | data formatting | bytes 1179648 | tf_op jit(solution)/shard_map/convert_element_type | solution.py:60
  (40 shorter events, 3.2 us)
Async XLA Ops:
  0.0 84.3 %copy-start = (bf16[1,72,72]{2,1,0:T(8,128)(2,1)S(1)}, bf16[1,72,72]{2,1,0:T(8,128)(2,1)}, u32[]{:S(2)}) copy-start(bf16[1,72,72]{2,1,0:T(8,128)(2,1)} %param.9) | copy-start | bytes 31108
  0.0 7.8 %copy-start.1 = (bf16[4,72,8,128]{3,2,1,0:T(8,128)(2,1)S(1)}, bf16[4,72,8,128]{3,2,1,0:T(8,128)(2,1)}, u32[]{:S(2)}) copy-start(bf16[4,72,8,128]{3,2,1,0:T(8,128)(2,1)} %param.6) | copy-start | bytes 1769476
  1.2 6.5 %collective-permute-start.1 = (bf16[4,72,1,128]{3,1,2,0:T(8,128)(2,1)S(1)}, bf16[4,72,1,128]{3,1,2,0:T(8,128)(2,1)S(1)}, u32[]{:S(2)}, u32[]{:S(2)}) collective-permute-start(bf16[4,72,1,128]{3,1,2,0:T(8,128)(2,1)S(1)} %get-tuple-element.18), channel_id=1, source_target_pairs={{0,8},{8,16},{16,24},{24,0},{1,9},{9,17},{17,25},{25,1},{2,10},{10... | collective-permute-start | bytes 221192 | tf_op jit(solution)/shard_map/ppermute | solution.py:16
  4.2 5.1 %collective-permute-start = (bf16[4,72,1,128]{3,1,2,0:T(8,128)(2,1)S(1)}, bf16[4,72,1,128]{3,1,2,0:T(8,128)(2,1)S(1)}, u32[]{:S(2)}, u32[]{:S(2)}) collective-permute-start(bf16[4,72,1,128]{3,1,2,0:T(8,128)(2,1)S(1)} %get-tuple-element.17), channel_id=1, source_target_pairs={{8,0},{16,8},{24,16},{0,24},{9,1},{17,9},{25,17},{1,25},{10,2},{18... | collective-permute-start | bytes 221192 | tf_op jit(solution)/shard_map/ppermute | solution.py:18
  10.4 4.1 %copy-start.3 = (bf16[2,72,8,128]{3,2,1,0:T(8,128)(2,1)S(1)}, bf16[2,72,8,128]{3,2,1,0:T(8,128)(2,1)}, u32[]{:S(2)}) copy-start(bf16[2,72,8,128]{3,2,1,0:T(8,128)(2,1)} %param.7) | copy-start | bytes 884740
  11.9 3.6 %collective-permute-start.2 = (bf16[4,72,10,1]{1,0,3,2:T(4,128)(2,1)S(1)}, bf16[4,72,10,1]{1,0,3,2:T(4,128)(2,1)S(1)}, u32[]{:S(2)}, u32[]{:S(2)}) collective-permute-start(bf16[4,72,10,1]{1,0,3,2:T(4,128)(2,1)S(1)} %copy.42), channel_id=1, source_target_pairs={{1,0},{2,1},{3,2},{4,3},{5,4},{6,5},{7,6},{0,7},{9,8},{10,9},{11,1... | collective-permute-start | bytes 17288 | tf_op jit(solution)/shard_map/ppermute | solution.py:18
  14.5 4.9 %collective-permute-start.3 = (bf16[4,72,10,1]{1,0,3,2:T(4,128)(2,1)S(1)}, bf16[4,72,10,1]{1,0,3,2:T(4,128)(2,1)S(1)}, u32[]{:S(2)}, u32[]{:S(2)}) collective-permute-start(bf16[4,72,10,1]{1,0,3,2:T(4,128)(2,1)S(1)} %copy.44), channel_id=1, source_target_pairs={{0,1},{1,2},{2,3},{3,4},{4,5},{5,6},{6,7},{7,0},{8,9},{9,10},{10,1... | collective-permute-start | bytes 17288 | tf_op jit(solution)/shard_map/ppermute | solution.py:16
  20.6 4.8 %copy-start.4 = (s32[1,8]{1,0:T(1,128)S(1)}, s32[1,8]{1,0:T(1,128)}, u32[]{:S(2)}) copy-start(s32[1,8]{1,0:T(1,128)} %param.8) | copy-start | bytes 100
  23.1 4.6 %collective-permute-start.4 = (bf16[4,72,1,128]{3,1,2,0:T(8,128)(2,1)S(1)}, bf16[4,72,1,128]{3,1,2,0:T(8,128)(2,1)S(1)}, u32[]{:S(2)}, u32[]{:S(2)}) collective-permute-start(bf16[4,72,1,128]{3,1,2,0:T(8,128)(2,1)S(1)} %get-tuple-element.16), channel_id=1, source_target_pairs={{8,0},{16,8},{24,16},{0,24},{9,1},{17,9},{25,17},{1,25},{10,2},{18... | collective-permute-start | bytes 221192 | tf_op jit(solution)/shard_map/ppermute | solution.py:18
  25.4 5.3 %collective-permute-start.5 = (bf16[4,72,1,128]{3,1,2,0:T(8,128)(2,1)S(1)}, bf16[4,72,1,128]{3,1,2,0:T(8,128)(2,1)S(1)}, u32[]{:S(2)}, u32[]{:S(2)}) collective-permute-start(bf16[4,72,1,128]{3,1,2,0:T(8,128)(2,1)S(1)} %get-tuple-element.15), channel_id=1, source_target_pairs={{0,8},{8,16},{16,24},{24,0},{1,9},{9,17},{17,25},{25,1},{2,10},{10... | collective-permute-start | bytes 221192 | tf_op jit(solution)/shard_map/ppermute | solution.py:16
  33.3 1.4 %collective-permute-start.6 = (bf16[4,72,10,1]{1,0,3,2:T(4,128)(2,1)S(1)}, bf16[4,72,10,1]{1,0,3,2:T(4,128)(2,1)S(1)}, u32[]{:S(2)}, u32[]{:S(2)}) collective-permute-start(bf16[4,72,10,1]{1,0,3,2:T(4,128)(2,1)S(1)} %copy.47), channel_id=1, source_target_pairs={{1,0},{2,1},{3,2},{4,3},{5,4},{6,5},{7,6},{0,7},{9,8},{10,9},{11,1... | collective-permute-start | bytes 17288 | tf_op jit(solution)/shard_map/ppermute | solution.py:18
  33.7 4.9 %collective-permute-start.7 = (bf16[4,72,10,1]{1,0,3,2:T(4,128)(2,1)S(1)}, bf16[4,72,10,1]{1,0,3,2:T(4,128)(2,1)S(1)}, u32[]{:S(2)}, u32[]{:S(2)}) collective-permute-start(bf16[4,72,10,1]{1,0,3,2:T(4,128)(2,1)S(1)} %copy.49), channel_id=1, source_target_pairs={{0,1},{1,2},{2,3},{3,4},{4,5},{5,6},{6,7},{7,0},{8,9},{9,10},{10,1... | collective-permute-start | bytes 17288 | tf_op jit(solution)/shard_map/ppermute | solution.py:16
  42.2 4.4 %collective-permute-start.8 = (bf16[4,72,1,128]{3,1,2,0:T(8,128)(2,1)S(1)}, bf16[4,72,1,128]{3,1,2,0:T(8,128)(2,1)S(1)}, u32[]{:S(2)}, u32[]{:S(2)}) collective-permute-start(bf16[4,72,1,128]{3,1,2,0:T(8,128)(2,1)S(1)} %get-tuple-element.14), channel_id=1, source_target_pairs={{8,0},{16,8},{24,16},{0,24},{9,1},{17,9},{25,17},{1,25},{10,2},{18... | collective-permute-start | bytes 221192 | tf_op jit(solution)/shard_map/ppermute | solution.py:18
  43.3 5.3 %collective-permute-start.9 = (bf16[4,72,1,128]{3,1,2,0:T(8,128)(2,1)S(1)}, bf16[4,72,1,128]{3,1,2,0:T(8,128)(2,1)S(1)}, u32[]{:S(2)}, u32[]{:S(2)}) collective-permute-start(bf16[4,72,1,128]{3,1,2,0:T(8,128)(2,1)S(1)} %get-tuple-element.13), channel_id=1, source_target_pairs={{0,8},{8,16},{16,24},{24,0},{1,9},{9,17},{17,25},{25,1},{2,10},{10... | collective-permute-start | bytes 221192 | tf_op jit(solution)/shard_map/ppermute | solution.py:16
  49.3 1.4 %collective-permute-start.10 = (bf16[4,72,10,1]{1,0,3,2:T(4,128)(2,1)S(1)}, bf16[4,72,10,1]{1,0,3,2:T(4,128)(2,1)S(1)}, u32[]{:S(2)}, u32[]{:S(2)}) collective-permute-start(bf16[4,72,10,1]{1,0,3,2:T(4,128)(2,1)S(1)} %copy.51), channel_id=1, source_target_pairs={{1,0},{2,1},{3,2},{4,3},{5,4},{6,5},{7,6},{0,7},{9,8},{10,9},{11,1... | collective-permute-start | bytes 17288 | tf_op jit(solution)/shard_map/ppermute | solution.py:18
  49.7 4.9 %collective-permute-start.11 = (bf16[4,72,10,1]{1,0,3,2:T(4,128)(2,1)S(1)}, bf16[4,72,10,1]{1,0,3,2:T(4,128)(2,1)S(1)}, u32[]{:S(2)}, u32[]{:S(2)}) collective-permute-start(bf16[4,72,10,1]{1,0,3,2:T(4,128)(2,1)S(1)} %copy.53), channel_id=1, source_target_pairs={{0,1},{1,2},{2,3},{3,4},{4,5},{5,6},{6,7},{7,0},{8,9},{9,10},{10,1... | collective-permute-start | bytes 17288 | tf_op jit(solution)/shard_map/ppermute | solution.py:16
  59.0 9.3 %copy-start.2 = (bf16[16,72,72]{2,1,0:T(8,128)(2,1)S(1)}, bf16[16,72,72]{2,1,0:T(8,128)(2,1)}, u32[]{:S(2)}) copy-start(bf16[16,72,72]{2,1,0:T(8,128)(2,1)} %param.11) | copy-start | bytes 497668
  64.1 20.2 %all-to-all-start = ((bf16[8,4,72,1,128]{4,2,1,3,0:T(8,128)(2,1)}), bf16[8,4,72,1,128]{4,2,1,3,0:T(8,128)(2,1)S(1)}, u32[]{:S(2)}, u32[]{:S(2)}) async-start(bf16[8,4,72,1,128]{4,2,1,3,0:T(8,128)(2,1)} %fusion.33), calls=%async_computation | async-start | bytes 1179648 | tf_op jit(solution)/shard_map/all_to_all | solution.py:51
